TPU v7x, 512 devices: a whole 4x4x16 slice. The times are simulated.
512 devices in a mesh: seq: 64 (over x, z), tp: 8 (over y, core).
Axes of the slice: x: 4, y: 4, z: 16, core: 2. Of those that a mesh axis runs over, the one named last changes fastest.
Arguments:
- queries: bfloat16 [64, 4, 8192], P('seq', None, 'tp'), may hold values from -40 to 40
- new_keys: bfloat16 [64, 4, 1024], P('seq', None, 'tp'), may hold values from -6 to 6
- new_values: bfloat16 [64, 4, 1024], P('seq', None, 'tp'), may hold values from -6 to 6
- prefix_keys: bfloat16 [8, 12288, 1024], P(None, 'seq', 'tp'), may hold values from -8 to 8
- prefix_values: bfloat16 [8, 12288, 1024], P(None, 'seq', 'tp'), may hold values from -6 to 6
- page_keys: bfloat16 [1024, 64, 1024], P('seq', None, 'tp'), may hold values from -6 to 6
- page_values: bfloat16 [1024, 64, 1024], P('seq', None, 'tp'), may hold values from -6 to 6
- out_weight: bfloat16 [8192, 8192], P('tp', 'seq'), may hold values from -0.5 to 0.5
- group_of: int32 [64], replicated, may hold values from 0 to 7, as said below
- prefix_len: int32 [8], replicated, may hold values from 2 to 12288, as said below
- total_len: int32 [64], replicated, may hold values from 3 to 16384, as said below
- page_owner: int32 [1024], P('seq'), may hold values from 0 to 63, as said below
- page_slot: int32 [1024], P('seq'), may hold values from 0 to 63, as said below
- new_valid: int32 [64, 4], replicated, may hold values from 0 to 1, as said below
Outputs:
- attn_out: bfloat16 [256, 8192], P('tp', 'seq')
Inputs may be any that keep to these rules, and one draw needn't show every extreme that they name: `group_of`: every one of the 8 groups has at least one request. `prefix_len`: some group's prefix holds exactly 12288 tokens. `page_owner`: every request owns at least one page and at most 64 pages; one request owns exactly 64. `page_slot`: the pages of one request carry the slots 0, 1, 2 and so on, each once. A request's pages are full except the one of its highest slot, which holds 1 to 64 tokens; total_len is its group's prefix length plus these tokens. `new_valid`: each row is a run of ones followed by zeros, and its first entry is one.
All inputs are finite; a program needn't handle non-finite values.
Results may differ from a plain program's by a relative error of at most 0.022.
Values may be sent and summed in bfloat16 or wider, within the bound.
No kernel may reach another device: no remote copies, remote signals or barrier semaphores. Data moves between devices by JAX's collectives and lax.ppermute only.
A program may use at most 192 MiB of HBM per device.

v0:
```python
import jax
import jax.numpy as jnp
from jax import lax
from jax.sharding import PartitionSpec as P

HEAD_DIM = 128
HPK = 8
GROUPS = 8
NEW = 4
NEG = -1e30


def merged(part, axis, combine):
    gathered = jax.tree.map(lambda a: lax.all_gather(a, axis), part)

    def take(source):
        return jax.tree.map(lambda a: lax.dynamic_index_in_dim(a, source, 0, False), gathered)

    return lax.fori_loop(
        1, lax.axis_size(axis), lambda source, state: combine(state, take(source)), take(0)
    )


def softmax_part(scores, key_mask):
    masked = jnp.where(key_mask, scores, NEG)
    row_peak = jnp.max(masked, axis=-1)
    weights = jnp.where(key_mask, jnp.exp(masked - row_peak[..., None]), 0.0)
    return (row_peak, jnp.sum(weights, axis=-1), weights.astype(jnp.bfloat16))


def combine(first_part, second_part):
    peak_a, total_a, out_a = first_part
    peak_b, total_b, out_b = second_part
    top_peak = jnp.maximum(peak_a, peak_b)
    factor_a = jnp.exp(peak_a - top_peak)
    factor_b = jnp.exp(peak_b - top_peak)
    return (
        top_peak,
        total_a * factor_a + total_b * factor_b,
        out_a * factor_a[..., None] + out_b * factor_b[..., None],
    )


def local(
    queries,
    new_keys,
    new_values,
    prefix_keys,
    prefix_values,
    page_keys,
    page_values,
    out_weight,
    group_of,
    prefix_len,
    total_len,
    page_owner,
    page_slot,
    new_valid,
):
    req_dev = queries.shape[0]
    seq_count = lax.axis_size("seq")
    requests = req_dev * seq_count
    kv_local = new_keys.shape[2] // HEAD_DIM
    heads_local = kv_local * HPK
    score_scale = HEAD_DIM ** (-0.5)
    seq_idx = lax.axis_index("seq")
    gathered = lax.all_gather(queries, "seq", axis=0, tiled=True)
    query_all = gathered.reshape(requests, NEW, kv_local, HPK, HEAD_DIM)
    group_hot = group_of[:, None] == jnp.arange(GROUPS, dtype=jnp.int32)[None, :]
    own_prefix = jnp.sum(jnp.where(group_hot, prefix_len[None, :], 0), axis=1)
    suffix_len = total_len - own_prefix
    pre_dev = prefix_keys.shape[1]
    positions = seq_idx * pre_dev + jnp.arange(pre_dev, dtype=jnp.int32)
    pre_keys = prefix_keys.reshape(GROUPS, pre_dev, kv_local, HEAD_DIM)
    pre_values = prefix_values.reshape(GROUPS, pre_dev, kv_local, HEAD_DIM)
    partial_value = (
        jnp.full((requests, NEW, kv_local, HPK), NEG, jnp.float32),
        jnp.zeros((requests, NEW, kv_local, HPK), jnp.float32),
        jnp.zeros((requests, NEW, kv_local, HPK, HEAD_DIM), jnp.float32),
    )
    for group_idx in range(GROUPS):
        scores = (
            jnp.einsum(
                "rjkhd,ikd->rjkhi",
                query_all,
                pre_keys[group_idx],
                preferred_element_type=jnp.float32,
            )
            * score_scale
        )
        member = group_hot[:, group_idx]
        live_keys = positions < prefix_len[group_idx]
        key_mask = member[:, None, None, None, None] & live_keys[None, None, None, None, :]
        row_peak, row_total, weights = softmax_part(scores, key_mask)
        values = jnp.einsum(
            "rjkhi,ikd->rjkhd", weights, pre_values[group_idx], preferred_element_type=jnp.float32
        )
        chosen = member[:, None, None, None]
        partial_value = (
            jnp.where(chosen, row_peak, partial_value[0]),
            jnp.where(chosen, row_total, partial_value[1]),
            jnp.where(chosen[..., None], values, partial_value[2]),
        )
    prefix_part = partial_value
    page_count = page_keys.shape[0]
    page_len = page_keys.shape[1]
    key_pages = page_keys.reshape(page_count, page_len, kv_local, HEAD_DIM)
    value_pages = page_values.reshape(page_count, page_len, kv_local, HEAD_DIM)
    owner_hot = page_owner[:, None] == jnp.arange(requests, dtype=jnp.int32)[None, :]
    own_suffix = jnp.sum(jnp.where(owner_hot, suffix_len[None, :], 0), axis=1)
    page_queries = jnp.take(query_all, page_owner, axis=0)
    scores = (
        jnp.einsum("pjkhd,pikd->pjkhi", page_queries, key_pages, preferred_element_type=jnp.float32)
        * score_scale
    )
    offsets = page_slot[:, None] * page_len + jnp.arange(page_len, dtype=jnp.int32)[None, :]
    live_keys = offsets < own_suffix[:, None]
    page_peak, page_total, weights = softmax_part(scores, live_keys[:, None, None, None, :])
    page_out = jnp.einsum(
        "pjkhi,pikd->pjkhd", weights, value_pages, preferred_element_type=jnp.float32
    )
    owner_wide = owner_hot[:, :, None, None, None]
    device_peak = jnp.max(jnp.where(owner_wide, page_peak[:, None], NEG), axis=0)
    page_back = jnp.max(jnp.where(owner_wide, device_peak[None], NEG), axis=1)
    factor = jnp.exp(page_peak - page_back)
    owner_float = owner_hot.astype(jnp.float32)
    suffix_total = jnp.einsum(
        "pr,pjkh->rjkh", owner_float, page_total * factor, precision=lax.Precision.HIGHEST
    )
    suffix_out = jnp.einsum(
        "pr,pjkhd->rjkhd",
        owner_float,
        page_out * factor[..., None],
        precision=lax.Precision.HIGHEST,
    )
    partial_value = combine(prefix_part, (device_peak, suffix_total, suffix_out))
    row_start = seq_idx * req_dev
    local_queries = queries.reshape(req_dev, NEW, kv_local, HPK, HEAD_DIM)
    local_keys = new_keys.reshape(req_dev, NEW, kv_local, HEAD_DIM)
    local_values = new_values.reshape(req_dev, NEW, kv_local, HEAD_DIM)
    valid_local = lax.dynamic_slice_in_dim(new_valid, row_start, req_dev, 0)
    scores = (
        jnp.einsum(
            "rjkhd,rikd->rjkhi", local_queries, local_keys, preferred_element_type=jnp.float32
        )
        * score_scale
    )
    causal = jnp.arange(NEW, dtype=jnp.int32)[None, :] <= jnp.arange(NEW, dtype=jnp.int32)[:, None]
    key_mask = causal[None, :, None, None, :] & (valid_local[:, None, None, None, :] == 1)
    row_peak, row_total, weights = softmax_part(scores, key_mask)
    new_out = jnp.einsum(
        "rjkhi,rikd->rjkhd", weights, local_values, preferred_element_type=jnp.float32
    )
    own_rows = (
        lax.dynamic_slice_in_dim(partial_value[0], row_start, req_dev, 0),
        lax.dynamic_slice_in_dim(partial_value[1], row_start, req_dev, 0),
        lax.dynamic_slice_in_dim(partial_value[2], row_start, req_dev, 0),
    )
    own_part = combine(own_rows, (row_peak, row_total, new_out))
    partial_value = (
        lax.dynamic_update_slice_in_dim(partial_value[0], own_part[0], row_start, 0),
        lax.dynamic_update_slice_in_dim(partial_value[1], own_part[1], row_start, 0),
        lax.dynamic_update_slice_in_dim(partial_value[2], own_part[2], row_start, 0),
    )
    final_peak, final_total, final_out = merged(partial_value, "seq", combine)
    valid_rows = new_valid.astype(jnp.float32)[:, :, None, None, None]
    attention = (final_out / final_total[..., None] * valid_rows).astype(jnp.bfloat16)
    attention = attention.reshape(requests * NEW, heads_local * HEAD_DIM)
    terms = jnp.dot(attention, out_weight, preferred_element_type=jnp.float32)
    summed = lax.psum_scatter(terms.astype(jnp.bfloat16), "tp", scatter_dimension=0, tiled=True)
    return summed


def solution(mesh):
    placed = (
        P("seq", None, "tp"),
        P("seq", None, "tp"),
        P("seq", None, "tp"),
        P(None, "seq", "tp"),
        P(None, "seq", "tp"),
        P("seq", None, "tp"),
        P("seq", None, "tp"),
        P("tp", "seq"),
        P(),
        P(),
        P(),
        P("seq"),
        P("seq"),
        P(),
    )
    return jax.shard_map(
        local, mesh=mesh, in_specs=placed, out_specs=P("tp", "seq"), check_vma=False
    )
```

profile of v0, /device:TPU:2, one launch (start us, length us, event | category | flops | bytes accessed | tf_op | source)
XLA Modules:
  0.0 936.6 jit_solution(16358263161853906716)
XLA Ops:
  12.8 106.3 %all_gather.25 = bf16[64,4,1024]{2,1,0:T(4,128)(2,1)S(1)} all-gather(bf16[1,4,1024]{2,1,0:T(4,128)(2,1)} %param.16), channel_id=1, replica_groups=mesh['seq'=64,'tp'=8] {'seq'}, dimensions={0}, use_global_device_ids=true | all-gather | bytes 532480 | tf_op jit(solution)/shard_map/all_gather | solution.py:67
  126.1 1.9 fusion.11
  129.3 1.9 fusion.10
  131.3 2.0 fusion.9
  149.6 2.3 fusion.58
  151.9 2.4 fusion.57
  154.3 2.3 fusion.56
  156.6 2.3 fusion.55
  159.0 2.3 fusion.54
  161.3 2.3 fusion.53
  163.6 2.3 fusion.52
  169.9 2.4 fusion.72
  185.5 3.2 fusion.150
  191.4 102.1 %all_gather.27 = f32[64,64,4,1,8]{1,4,3,2,0:T(8,128)S(1)} all-gather(f32[1,64,4,1,8]{1,4,3,2,0:T(8,128)S(1)} %bitcast.588), channel_id=1, replica_groups=mesh['seq'=64,'tp'=8] {'seq'}, dimensions={0}, use_global_device_ids=true | all-gather | bytes 532480 | tf_op jit(solution)/shard_map/all_gather | solution.py:14
  293.5 110.7 %all_gather.30 = f32[64,64,4,1,8]{1,4,3,2,0:T(8,128)} all-gather(f32[1,64,4,1,8]{1,4,3,2,0:T(8,128)S(1)} %bitcast.584), channel_id=1, replica_groups=mesh['seq'=64,'tp'=8] {'seq'}, dimensions={0}, use_global_device_ids=true | all-gather | bytes 532480 | tf_op jit(solution)/shard_map/all_gather | solution.py:14
  404.9 301.5 %all-gather.2.cloned.1.call-done = f32[64,64,4,1,8,128]{5,4,3,2,1,0:T(8,128)} async-done(((f32[1,64,4,1,8,128]{5,4,3,2,1,0:T(8,128)}), f32[64,64,4,1,8,128]{5,4,3,2,1,0:T(8,128)}) %all-gather.2.cloned.1.call-update) | async-done | bytes 67108880 | tf_op jit(solution)/shard_map/all_gather | solution.py:14
  707.8 184.2 %while.19 = (s32[]{:T(128)}, f32[64,4,1,8]{0,3,2,1:T(8,128)S(1)}, f32[64,4,1,8]{0,3,2,1:T(8,128)S(1)}, f32[64,4,1,8,128]{4,3,2,1,0:T(8,128)S(1)}, f32[64,64,4,1,...) while((s32[]{:T(128)}, f32[64,4,1,8]{0,3,2,1:T(8,128)S(1)}, ...), condition=%wide.region_25.26_spmd, body=%wide.region_24.25_spmd.sunk | while | flops 800773 | bytes 3301531 | solution.py:19
  708.8 1.9 fusion.182
  720.5 1.9 fusion.182
  726.3 1.9 fusion.182
  741.0 1.9 fusion.182
  761.4 1.9 fusion.182
  776.0 1.9 fusion.182
  781.9 1.9 fusion.182
  796.5 1.9 fusion.182
  817.0 1.9 fusion.182
  831.6 1.9 fusion.182
  837.4 1.9 fusion.182
  852.0 1.9 fusion.182
  872.5 1.9 fusion.182
  887.1 1.9 fusion.182
  893.6 36.2 %reduce-scatter.2.cloned.1.call-done = bf16[32,128]{1,0:T(8,128)(2,1)} async-done(((bf16[256,128]{1,0:T(8,128)(2,1)}), bf16[32,128]{1,0:T(8,128)(2,1)}) %reduce-scatter.2.cloned.1.call-update) | async-done | bytes 8208 | tf_op jit(solution)/shard_map/reduce_scatter | solution.py:170
  (631 shorter events, 207.6 us)
Async XLA Ops:
  6.5 162.1 %copy-start = (bf16[16,64,128]{2,1,0:T(8,128)(2,1)S(1)}, bf16[16,64,128]{2,1,0:T(8,128)(2,1)}, u32[]{:S(2)}) copy-start(bf16[16,64,128]{2,1,0:T(8,128)(2,1)} %param.22) | copy-start | bytes 786436
  6.5 699.9 %all-gather.2.cloned.1.call-start = ((), (), s32[]{:S(2)}) async-start(), calls=%async_computation.1 | async-start | bytes 68157440 | tf_op jit(solution)/shard_map/all_gather | solution.py:14
  119.1 7.0 copy-start.20
  122.5 5.5 copy-start.50
  122.5 6.7 copy-start.54
  122.6 10.8 %copy-start.61 = (pred[64]{0:T(512)(128)(4,1)}, pred[64]{0:T(512)(128)(4,1)S(1)}, u32[]{:S(2)}) copy-start(pred[64]{0:T(512)(128)(4,1)S(1)} %get-tuple-element.261) | copy-start | bytes 196
  122.6 13.3 %copy-start.65 = (pred[64]{0:T(512)(128)(4,1)}, pred[64]{0:T(512)(128)(4,1)S(1)}, u32[]{:S(2)}) copy-start(pred[64]{0:T(512)(128)(4,1)S(1)} %get-tuple-element.262) | copy-start | bytes 196
  122.6 14.6 %copy-start.69 = (pred[64]{0:T(512)(128)(4,1)}, pred[64]{0:T(512)(128)(4,1)S(1)}, u32[]{:S(2)}) copy-start(pred[64]{0:T(512)(128)(4,1)S(1)} %get-tuple-element.263) | copy-start | bytes 196
  122.6 17.2 %copy-start.73 = (pred[64]{0:T(512)(128)(4,1)}, pred[64]{0:T(512)(128)(4,1)S(1)}, u32[]{:S(2)}) copy-start(pred[64]{0:T(512)(128)(4,1)S(1)} %get-tuple-element.264) | copy-start | bytes 196
  122.6 18.7 %copy-start.77 = (pred[64]{0:T(512)(128)(4,1)}, pred[64]{0:T(512)(128)(4,1)S(1)}, u32[]{:S(2)}) copy-start(pred[64]{0:T(512)(128)(4,1)S(1)} %get-tuple-element.257) | copy-start | bytes 196
  128.1 17.9 %copy-start.14 = (f32[64,4,8]{0,2,1:T(8,128)}, f32[64,4,8]{0,2,1:T(8,128)S(1)}, u32[]{:S(2)}) copy-start(f32[64,4,8]{0,2,1:T(8,128)S(1)} %get-tuple-element.277) | copy-start | bytes 24580
  131.2 14.7 %copy-start.17 = (f32[64,4,8]{0,2,1:T(8,128)}, f32[64,4,8]{0,2,1:T(8,128)S(1)}, u32[]{:S(2)}) copy-start(f32[64,4,8]{0,2,1:T(8,128)S(1)} %get-tuple-element.279) | copy-start | bytes 24580
  142.5 7.0 copy-start.60
  165.9 9.4 %copy-start.4 = (bf16[64,4,8,192]{3,0,2,1:T(8,128)(2,1)S(1)}, bf16[64,4,8,192]{3,0,2,1:T(8,128)(2,1)}, u32[]{:S(2)}) copy-start(bf16[64,4,8,192]{3,0,2,1:T(8,128)(2,1)} %get-tuple-element.251) | copy-start | bytes 2359300
  169.9 7.1 copy-start.10
  169.9 7.1 copy-start.52
  184.9 5.4 copy-start.31
  184.9 5.4 copy-start.32
  184.9 5.4 copy-start.37
  184.9 5.4 copy-start.38
  184.9 5.4 copy-start.39
  184.9 5.4 copy-start.40
  184.9 5.4 copy-start.41
  184.9 5.4 copy-start.42
  184.9 5.4 copy-start.43
  185.0 5.4 copy-start.44
  185.0 5.4 copy-start.49
  185.0 5.4 copy-start.53
  185.1 5.7 copy-start.16
  185.1 5.7 copy-start.19
  189.9 739.8 %reduce-scatter.2.cloned.1.call-start = ((), (), s32[]{:S(2)}) async-start(), calls=%async_computation.2 | async-start | bytes 73728 | tf_op jit(solution)/shard_map/reduce_scatter | solution.py:170
  707.7 184.9 %copy-start.90 = (bf16[1024,128]{1,0:T(8,128)(2,1)S(1)}, bf16[1024,128]{1,0:T(8,128)(2,1)}, u32[]{:S(2)}) copy-start(bf16[1024,128]{1,0:T(8,128)(2,1)} %param.23) | copy-start | bytes 786436
  (62 other events, 195.6 us)
Sparse Core Ops, SparseCore 0:
  190.1 516.3 all-gather.1
  893.7 36.0 reduce-scatter.1
where the time goes:
time: 943 us; the launch traced here: 937 us
  waiting for transfers between devices  338 us (36%)
  blocking collectives  319 us (34%)
  other arithmetic  209 us (22%)
  local copies, waits for them, and re-layouts  29.6 us (3%)
  matrix products  23.3 us (2%)
  between operations  14.7 us (2%)
    all_gather x1, waiting for transfers between devices, merged(): gathered = jax.tree.map(lambda a: lax.all_gather(a, axis), part)  302 us
    all_gather x2, blocking collectives, merged(): gathered = jax.tree.map(lambda a: lax.all_gather(a, axis), part)  213 us
    add x63, other arithmetic, combine(): out_a * factor_a[..., None] + out_b * factor_b[..., None]  119 us
    all_gather x1, blocking collectives, local(): gathered = lax.all_gather(queries, 'seq', axis=0, tiled=True)  106 us
    mul x63, other arithmetic, combine(): out_b * factor_b[..., None]  46.8 us
    reduce_scatter x1, waiting for transfers between devices, local(): lax.psum_scatter(terms.astype(jnp.bfloat16), 'tp', scatter_dimension=0, t...  36.2 us
  transfers between devices with their start and end apart: 2, of which 2 were waited for; matrix products, arithmetic and copies ran while one was open for 0% of the time, Pallas kernels for 0%

commit v1 on v0

--- a/solution.py
+++ b/solution.py
@@ -64,7 +64,15 @@
     heads_local = kv_local * HPK
     score_scale = HEAD_DIM ** (-0.5)
     seq_idx = lax.axis_index("seq")
-    gathered = lax.all_gather(queries, "seq", axis=0, tiled=True)
+    gathered = jnp.concatenate(
+        lax.all_to_all(
+            jnp.stack([queries for _ in range(lax.axis_size("seq"))], axis=0),
+            "seq",
+            split_axis=0,
+            concat_axis=0,
+        ),
+        axis=0,
+    )
     query_all = gathered.reshape(requests, NEW, kv_local, HPK, HEAD_DIM)
     group_hot = group_of[:, None] == jnp.arange(GROUPS, dtype=jnp.int32)[None, :]
     own_prefix = jnp.sum(jnp.where(group_hot, prefix_len[None, :], 0), axis=1)

time: 943 us -> 857 us (0.909)
  blocking collectives: 319 us -> 214 us
  starting transfers between devices: 0.04 us -> 18.7 us
    all_gather x1 -> x0, blocking collectives: 106 us -> none  [local(): gathered = lax.all_gather(queries, 'seq', axis=0, tiled=True)]
    all_to_all x0 -> x1, starting transfers between devices: none -> 18.6 us  [local(): lax.all_to_all(jnp.stack([queries for _ in range(lax.axis_size('seq'))],...]
    all_to_all x0 -> x1, waiting for transfers between devices: none -> 11.5 us  [local(): lax.all_to_all(jnp.stack([queries for _ in range(lax.axis_size('seq'))],...]
  transfers between devices with their start and end apart: 2 -> 3, of which waited for: 2 -> 3; matrix products, arithmetic and copies ran while one was open for 0% -> 3% of each run, Pallas kernels for 0% -> 0%
where the time goes in v1:
time: 857 us; the launch traced here: 850 us
  waiting for transfers between devices  347 us (40%)
  blocking collectives  214 us (25%)
  other arithmetic  204 us (24%)
  local copies, waits for them, and re-layouts  30.6 us (4%)
  starting transfers between devices  18.7 us (2%)
  matrix products  17.8 us (2%)
  between operations  14.3 us (2%)
    all_gather x1, waiting for transfers between devices, merged(): gathered = jax.tree.map(lambda a: lax.all_gather(a, axis), part)  299 us
    all_gather x2, blocking collectives, merged(): gathered = jax.tree.map(lambda a: lax.all_gather(a, axis), part)  214 us
    add x63, other arithmetic, combine(): out_a * factor_a[..., None] + out_b * factor_b[..., None]  119 us
    mul x63, other arithmetic, combine(): out_b * factor_b[..., None]  46.8 us
    reduce_scatter x1, waiting for transfers between devices, local(): lax.psum_scatter(terms.astype(jnp.bfloat16), 'tp', scatter_dimension=0, t...  36.1 us
    all_to_all x1, starting transfers between devices, local(): lax.all_to_all(jnp.stack([queries for _ in range(lax.axis_size('seq'))],...  18.6 us
  transfers between devices with their start and end apart: 3, of which 3 were waited for; matrix products, arithmetic and copies ran while one was open for 3% of the time, Pallas kernels for 0%

profile of v1, /device:TPU:2, one launch (start us, length us, event | category | flops | bytes accessed | tf_op | source)
XLA Modules:
  0.0 849.6 jit_solution(7345891739126153928)
XLA Ops:
  8.2 18.6 %all-to-all-start = ((bf16[64,1,4,1024]{3,2,1,0:T(4,128)(2,1)}), bf16[64,1,4,1024]{3,2,1,0:T(4,128)(2,1)S(1)}, u32[]{:S(2)}, u32[]{:S(2)}) async-start(bf16[64,1,4,1024]{3,2,1,0:T(4,128)(2,1)} %stack.2), calls=%async_computation | async-start | bytes 1048576 | tf_op jit(solution)/shard_map/all_to_all | solution.py:68
  47.0 11.5 %all-to-all-done = bf16[64,1,4,1024]{3,2,1,0:T(4,128)(2,1)S(1)} async-done(((bf16[64,1,4,1024]{3,2,1,0:T(4,128)(2,1)}), bf16[64,1,4,1024]{3,2,1,0:T(4,128)(2,1)S(1)}, u32[]{:S(2)}, u32[]{:S(2)}) %all-to-all-start) | async-done | bytes 524320 | tf_op jit(solution)/shard_map/all_to_all | solution.py:68
  67.7 2.3 fusion.59
  72.9 2.3 fusion.56
  75.3 2.3 fusion.55
  77.6 2.3 fusion.54
  79.9 2.5 fusion.53
  99.8 3.3 fusion.150
  105.7 103.1 %all_gather.23 = f32[64,64,4,1,8]{1,4,3,2,0:T(8,128)S(1)} all-gather(f32[1,64,4,1,8]{1,4,3,2,0:T(8,128)S(1)} %bitcast.589), channel_id=1, replica_groups=mesh['seq'=64,'tp'=8] {'seq'}, dimensions={0}, use_global_device_ids=true | all-gather | bytes 532480 | tf_op jit(solution)/shard_map/all_gather | solution.py:14
  208.7 110.8 %all_gather.26 = f32[64,64,4,1,8]{1,4,3,2,0:T(8,128)} all-gather(f32[1,64,4,1,8]{1,4,3,2,0:T(8,128)S(1)} %bitcast.585), channel_id=1, replica_groups=mesh['seq'=64,'tp'=8] {'seq'}, dimensions={0}, use_global_device_ids=true | all-gather | bytes 532480 | tf_op jit(solution)/shard_map/all_gather | solution.py:14
  320.3 299.2 %all-gather.2.cloned.1.call-done = f32[64,64,4,1,8,128]{5,4,3,2,1,0:T(8,128)} async-done(((f32[1,64,4,1,8,128]{5,4,3,2,1,0:T(8,128)}), f32[64,64,4,1,8,128]{5,4,3,2,1,0:T(8,128)}) %all-gather.2.cloned.1.call-update) | async-done | bytes 67108880 | tf_op jit(solution)/shard_map/all_gather | solution.py:14
  620.8 184.2 %while.19 = (s32[]{:T(128)}, f32[64,4,1,8]{0,3,2,1:T(8,128)S(1)}, f32[64,4,1,8]{0,3,2,1:T(8,128)S(1)}, f32[64,4,1,8,128]{4,3,2,1,0:T(8,128)S(1)}, f32[64,64,4,1,...) while((s32[]{:T(128)}, f32[64,4,1,8]{0,3,2,1:T(8,128)S(1)}, ...), condition=%wide.region_25.26_spmd, body=%wide.region_24.25_spmd.sunk | while | flops 800773 | bytes 3301531 | solution.py:19
  621.8 1.9 fusion.182
  624.7 1.9 fusion.182
  627.7 1.9 fusion.182
  630.6 1.9 fusion.182
  633.5 1.9 fusion.182
  636.4 1.9 fusion.182
  639.4 1.9 fusion.182
  642.3 1.9 fusion.182
  648.1 1.9 fusion.182
  662.7 1.9 fusion.182
  683.2 1.9 fusion.182
  697.8 1.9 fusion.182
  703.7 1.9 fusion.182
  718.3 1.9 fusion.182
  738.7 1.9 fusion.182
  753.3 1.9 fusion.182
  759.2 1.9 fusion.182
  773.8 1.9 fusion.182
  794.3 1.9 fusion.182
  806.6 36.1 %reduce-scatter.2.cloned.1.call-done = bf16[32,128]{1,0:T(8,128)(2,1)} async-done(((bf16[256,128]{1,0:T(8,128)(2,1)}), bf16[32,128]{1,0:T(8,128)(2,1)}) %reduce-scatter.2.cloned.1.call-update) | async-done | bytes 8208 | tf_op jit(solution)/shard_map/reduce_scatter | solution.py:178
  (557 shorter events, 201.5 us)
Async XLA Ops:
  6.5 78.0 %copy-start = (bf16[16,64,128]{2,1,0:T(8,128)(2,1)S(1)}, bf16[16,64,128]{2,1,0:T(8,128)(2,1)}, u32[]{:S(2)}) copy-start(bf16[16,64,128]{2,1,0:T(8,128)(2,1)} %param.22) | copy-start | bytes 786436
  6.5 52.8 %copy-start.8 = (bf16[8,192,128]{2,1,0:T(8,128)(2,1)S(1)}, bf16[8,192,128]{2,1,0:T(8,128)(2,1)}, u32[]{:S(2)}) copy-start(bf16[8,192,128]{2,1,0:T(8,128)(2,1)} %param.19) | copy-start | bytes 1179652
  8.2 50.3 %all-to-all-start = ((bf16[64,1,4,1024]{3,2,1,0:T(4,128)(2,1)}), bf16[64,1,4,1024]{3,2,1,0:T(4,128)(2,1)S(1)}, u32[]{:S(2)}, u32[]{:S(2)}) async-start(bf16[64,1,4,1024]{3,2,1,0:T(4,128)(2,1)} %stack.2), calls=%async_computation | async-start | bytes 1048576 | tf_op jit(solution)/shard_map/all_to_all | solution.py:68
  26.9 592.6 %all-gather.2.cloned.1.call-start = ((), (), s32[]{:S(2)}) async-start(), calls=%async_computation.2 | async-start | bytes 68157440 | tf_op jit(solution)/shard_map/all_gather | solution.py:14
  34.2 31.9 %copy-start.28 = (pred[64]{0:T(512)(128)(4,1)}, pred[64]{0:T(512)(128)(4,1)S(1)}, u32[]{:S(2)}) copy-start(pred[64]{0:T(512)(128)(4,1)S(1)} %get-tuple-element.258) | copy-start | bytes 196
  34.2 31.9 %copy-start.30 = (pred[64]{0:T(512)(128)(4,1)}, pred[64]{0:T(512)(128)(4,1)S(1)}, u32[]{:S(2)}) copy-start(pred[64]{0:T(512)(128)(4,1)S(1)} %get-tuple-element.259) | copy-start | bytes 196
  34.2 31.9 %copy-start.33 = (pred[64]{0:T(512)(128)(4,1)}, pred[64]{0:T(512)(128)(4,1)S(1)}, u32[]{:S(2)}) copy-start(pred[64]{0:T(512)(128)(4,1)S(1)} %get-tuple-element.260) | copy-start | bytes 196
  34.2 31.9 %copy-start.37 = (pred[64]{0:T(512)(128)(4,1)}, pred[64]{0:T(512)(128)(4,1)S(1)}, u32[]{:S(2)}) copy-start(pred[64]{0:T(512)(128)(4,1)S(1)} %get-tuple-element.261) | copy-start | bytes 196
  34.2 31.9 %copy-start.39 = (pred[64]{0:T(512)(128)(4,1)}, pred[64]{0:T(512)(128)(4,1)S(1)}, u32[]{:S(2)}) copy-start(pred[64]{0:T(512)(128)(4,1)S(1)} %get-tuple-element.262) | copy-start | bytes 196
  34.3 31.9 %copy-start.41 = (pred[64]{0:T(512)(128)(4,1)}, pred[64]{0:T(512)(128)(4,1)S(1)}, u32[]{:S(2)}) copy-start(pred[64]{0:T(512)(128)(4,1)S(1)} %get-tuple-element.263) | copy-start | bytes 196
  34.3 31.9 %copy-start.43 = (pred[64]{0:T(512)(128)(4,1)}, pred[64]{0:T(512)(128)(4,1)S(1)}, u32[]{:S(2)}) copy-start(pred[64]{0:T(512)(128)(4,1)S(1)} %get-tuple-element.264) | copy-start | bytes 196
  34.3 31.9 %copy-start.45 = (pred[64]{0:T(512)(128)(4,1)}, pred[64]{0:T(512)(128)(4,1)S(1)}, u32[]{:S(2)}) copy-start(pred[64]{0:T(512)(128)(4,1)S(1)} %get-tuple-element.257) | copy-start | bytes 196
  35.3 32.1 %copy-start.35 = (pred[16,64]{1,0:T(8,128)(4,1)}, pred[16,64]{1,0:T(8,128)(4,1)S(1)}, u32[]{:S(2)}) copy-start(pred[16,64]{1,0:T(8,128)(4,1)S(1)} %add_compare_fusion) | copy-start | bytes 3076
  46.9 12.5 %copy-start.11 = (pred[64,192]{1,0:T(8,128)(4,1)}, pred[64,192]{1,0:T(8,128)(4,1)S(1)}, u32[]{:S(2)}) copy-start(pred[64,192]{1,0:T(8,128)(4,1)S(1)} %broadcast_and_fusion) | copy-start | bytes 36868
  99.1 5.2 copy-start.48
  99.1 5.2 copy-start.47
  99.1 5.4 copy-start.16
  99.1 5.5 copy-start.13
  99.1 5.5 copy-start.14
  99.1 5.5 copy-start.19
  99.1 5.5 copy-start.20
  99.2 5.5 copy-start.21
  99.2 5.5 copy-start.22
  99.2 5.5 copy-start.23
  99.2 5.5 copy-start.24
  99.2 5.5 copy-start.25
  99.2 5.5 copy-start.26
  99.2 5.5 copy-start.29
  99.2 5.5 copy-start.32
  99.2 5.5 copy-start.50
  104.3 738.5 %reduce-scatter.2.cloned.1.call-start = ((), (), s32[]{:S(2)}) async-start(), calls=%async_computation.3 | async-start | bytes 73728 | tf_op jit(solution)/shard_map/reduce_scatter | solution.py:178
  620.8 184.9 %copy-start.52 = (bf16[1024,128]{1,0:T(8,128)(2,1)S(1)}, bf16[1024,128]{1,0:T(8,128)(2,1)}, u32[]{:S(2)}) copy-start(bf16[1024,128]{1,0:T(8,128)(2,1)} %param.23) | copy-start | bytes 786436
  (25 other events, 41.0 us)
Sparse Core Ops, SparseCore 0:
  104.4 515.0 all-gather.1
  806.7 35.9 reduce-scatter.1
